TPU v7x, 32 devices: a whole 2x2x4 slice. The times are simulated.
32 devices in a mesh: row: 4 (over y, x), col: 4 (over z), layer: 2 (over core).
Axes of the slice: x: 2, y: 2, z: 4, core: 2. Of those that a mesh axis runs over, the one named last changes fastest.
Arguments:
- x_blocks: bfloat16 [64, 64, 4, 256], P('col', None, 'row'), may hold values from -1 to 1
- x_cols: int32 [64, 4, 4], P('col', 'row'), may hold values from 0 to 15, as said below
- x_count: int32 [64, 4], P('col', 'row'), may hold values from 1 to 4, as said below
- out_cols: int32 [64, 4, 8], P('col', 'row'), may hold values from 0 to 15, as said below
Outputs:
- product: float32 [64, 64, 4, 512], P('col', None, 'row', 'layer')
Inputs may be any that keep to these rules, and one draw needn't show every extreme that they name: `x_cols`: within one block row and tile the 4 column entries are distinct. For every tile column t, at least one block row R has x_count[R,t] = 4. `out_cols`: within one block row and tile the 8 column entries are distinct.
All inputs are finite; a program needn't handle non-finite values.
Results may differ from a plain program's by a relative error of at most 0.0003.
Values may be sent and summed in bfloat16 or wider, within the bound.
No kernel may reach another device: no remote copies, remote signals or barrier semaphores. Data moves between devices by JAX's collectives and lax.ppermute only.
A program may use at most 64 MiB of HBM per device.

v0:
```python
import jax
import jax.numpy as jnp
from jax import lax
from jax.sharding import PartitionSpec as P


def for_sending(x):
    return jax.tree.map(lambda a: a.astype(jnp.bfloat16) if a.dtype == jnp.float32 else a, x)


def from_behind(x, axis, by):
    devices = lax.axis_size(axis)
    return lax.ppermute(x, axis, [(i, (i + by) % devices) for i in range(devices)])


def accumulate(total, left, upper, wanted):
    a_vals, a_cols = left
    b_vals, b_cols = upper
    row_count, width, lanes = a_vals.shape
    slots = a_cols.shape[1]
    row_ids = lax.broadcasted_iota(jnp.int32, (1, 1, 1, row_count, 1), 3)
    take_row = a_cols[:, :, None, None, None] == row_ids
    take_slot = b_cols[None, None, None, :, :] == wanted[:, None, :, None, None]
    select = jnp.logical_and(take_row, take_slot).astype(jnp.bfloat16)
    blocks = b_vals.reshape(row_count, width, slots, width)
    picked = jnp.einsum("rpokq,kbqc->rpobc", select, blocks, preferred_element_type=jnp.float32)
    picked = picked.astype(jnp.bfloat16)
    factor = a_vals.reshape(row_count, width, slots, width)
    result = jnp.einsum("rapb,rpobc->raoc", factor, picked, preferred_element_type=jnp.float32)
    return total + result.reshape(row_count, width, -1)


def pick_if(flag, moved, kept):
    return (jnp.where(flag, moved[0], kept[0]), jnp.where(flag, moved[1], kept[1]))


def per_device(x_blocks, x_cols, x_count, out_cols):
    row_count, width, _, lanes = x_blocks.shape
    values = x_blocks[:, :, 0, :]
    slot_of_lane = lax.broadcasted_iota(jnp.int32, (1, 1, lanes), 2) // width
    values = jnp.where(slot_of_lane < x_count[:, :, None], values, jnp.zeros((), values.dtype))
    columns = x_cols[:, 0, :]
    wanted = out_cols[:, 0, :]
    groups = lax.axis_size("row")
    layers = lax.axis_size("layer")
    steps = groups // layers
    offset = lax.axis_index("layer") * steps
    total = jnp.zeros((row_count, width, wanted.shape[1] * width), jnp.float32)
    left = (values, columns)
    upper = (values, columns)
    left_dist = (lax.axis_index("col") + offset) % groups
    upper_dist = (lax.axis_index("row") + offset) % groups
    for bit in range((groups - 1).bit_length()):
        moved = from_behind((left[0], for_sending(left[1])), "row", groups - (1 << bit))
        left = pick_if(left_dist >> bit & 1 == 1, moved, left)
        moved = from_behind((upper[0], for_sending(upper[1])), "col", groups - (1 << bit))
        upper = pick_if(upper_dist >> bit & 1 == 1, moved, upper)

    def turn_next(step, carry):
        total, left, upper = carry
        total = accumulate(total, left, upper, wanted)
        left = from_behind((left[0], for_sending(left[1])), "row", groups - 1)
        upper = from_behind((upper[0], for_sending(upper[1])), "col", groups - 1)
        return (total, left, upper)

    total, left, upper = lax.fori_loop(0, steps - 1, turn_next, (total, left, upper))
    total = accumulate(total, left, upper, wanted)
    share = lax.psum_scatter(total, "layer", scatter_dimension=2, tiled=True)
    return share[:, :, None, :]


def solution(mesh):
    placed = (
        P("col", None, "row", None),
        P("col", "row", None),
        P("col", "row"),
        P("col", "row", None),
    )
    return jax.shard_map(
        per_device,
        mesh=mesh,
        in_specs=placed,
        out_specs=P("col", None, "row", "layer"),
        check_vma=False,
    )
```

profile of v0, /device:TPU:0, one launch (start us, length us, event | category | flops | bytes accessed | tf_op | source)
XLA Modules:
  0.0 130.9 jit_solution(17244395968474798329)
XLA Ops:
  6.5 0.0 reduce-scatter.2.cloned.1.call-start
  6.5 0.7 broadcast_compare_fusion.2
  7.3 1.1 bitcast_select_fusion
  8.4 3.9 %collective-permute-start = (bf16[16,64,256]{2,1,0:T(8,128)(2,1)S(1)}, bf16[16,64,256]{2,1,0:T(8,128)(2,1)S(1)}, u32[]{:S(2)}, u32[]{:S(2)}) collective-permute-start(bf16[16,64,256]{2,1,0:T(8,128)(2,1)S(1)} %bitcast_select_fusion), channel_id=1, source_target_pairs={{0,24},{8,0},{16,8},{24,16},{1,25},{9,1},{17,9},{25,17},{2,26},{10... | collective-permute-start | bytes 1572872 | tf_op jit(solution)/shard_map/ppermute | solution.py:13
  12.3 3.6 %collective-permute-start.6 = (bf16[16,64,256]{2,1,0:T(8,128)(2,1)S(1)}, bf16[16,64,256]{2,1,0:T(8,128)(2,1)S(1)}, u32[]{:S(2)}, u32[]{:S(2)}) collective-permute-start(bf16[16,64,256]{2,1,0:T(8,128)(2,1)S(1)} %bitcast_select_fusion), channel_id=1, source_target_pairs={{0,6},{2,0},{4,2},{6,4},{1,7},{3,1},{5,3},{7,5},{8,14},{10,8},{12,... | collective-permute-start | bytes 1572872 | tf_op jit(solution)/shard_map/ppermute | solution.py:13
  15.9 0.5 collective-permute-start.2
  16.4 0.4 collective-permute-start.4
  16.9 6.6 %collective-permute-done.2 = s32[16,4]{0,1:T(4,128)S(1)} collective-permute-done((s32[16,4]{0,1:T(4,128)}, s32[16,4]{0,1:T(4,128)S(1)}, u32[]{:S(2)}, u32[]{:S(2)}) %collective-permute-start.2) | collective-permute-done | bytes 288 | tf_op jit(solution)/shard_map/ppermute | solution.py:13
  23.5 3.3 %collective-permute-done.4 = s32[16,4]{0,1:T(4,128)S(1)} collective-permute-done((s32[16,4]{0,1:T(4,128)}, s32[16,4]{0,1:T(4,128)S(1)}, u32[]{:S(2)}, u32[]{:S(2)}) %collective-permute-start.4) | collective-permute-done | bytes 288 | tf_op jit(solution)/shard_map/ppermute | solution.py:13
  26.9 0.7 broadcast_select_fusion.6
  27.5 0.5 collective-permute-start.3
  28.0 0.8 copy.13
  28.8 1.5 %collective-permute-start.5 = (s32[16,4]{0,1:T(4,128)S(1)}, s32[16,4]{0,1:T(4,128)S(1)}, u32[]{:S(2)}, u32[]{:S(2)}) collective-permute-start(s32[16,4]{0,1:T(4,128)S(1)} %get-tuple-element.30), channel_id=1, source_target_pairs={{0,4},{2,6},{4,0},{6,2},{1,5},{3,7},{5,1},{7,3},{8,12},{10,14},{12... | collective-permute-start | bytes 776 | tf_op jit(solution)/shard_map/ppermute | solution.py:13
  30.3 0.9 collective-permute-done.3
  31.1 0.1 copy.11
  31.2 0.5 collective-permute-start.9
  31.8 1.5 %collective-permute-done.5 = s32[16,4]{0,1:T(4,128)S(1)} collective-permute-done((s32[16,4]{0,1:T(4,128)S(1)}, s32[16,4]{0,1:T(4,128)S(1)}, u32[]{:S(2)}, u32[]{:S(2)}) %collective-permute-start.5) | collective-permute-done | bytes 288 | tf_op jit(solution)/shard_map/ppermute | solution.py:13
  33.3 4.3 %collective-permute-start.10 = (s32[16,4]{0,1:T(4,128)S(1)}, s32[16,4]{0,1:T(4,128)S(1)}, u32[]{:S(2)}, u32[]{:S(2)}) collective-permute-start(s32[16,4]{0,1:T(4,128)S(1)} %broadcast_select_fusion.5), channel_id=1, source_target_pairs={{0,6},{2,0},{4,2},{6,4},{1,7},{3,1},{5,3},{7,5},{8,14},{10,8},{12,... | collective-permute-start | bytes 776 | tf_op jit(solution)/shard_map/while/body/eval_jaxpr/ppermute | solution.py:13
  37.6 0.1 iota_compare_fusion.1
  37.7 0.1 copy.12
  37.7 1.1 collective-permute-done.10
  38.9 0.1 copy.16
  39.0 0.4 broadcast_compare_fusion
  39.3 0.6 and_bitcast_fusion.1
  40.0 4.2 %copy.20 = pred[16,4,8,16,4,1]{3,0,4,5,2,1:T(8,128)(4,1)} copy(pred[16,4,8,16,4,1]{4,3,2,1,0,5:T(8,128)(4,1)S(1)} %and_bitcast_fusion.1) | data formatting | bytes 65536 | tf_op jit(solution)/shard_map/while/body/eval_jaxpr/and | solution.py:24
  44.2 0.0 collective-permute-done.9
  44.2 0.1 copy.15
  44.3 0.0 collective-permute-done
  44.3 0.0 collective-permute-done.6
  44.3 1.1 broadcast_select_fusion.2
  45.4 0.9 collective-permute-start.7
  46.3 0.1 iota_compare_fusion
  46.4 1.6 %collective-permute-start.1 = (bf16[16,64,256]{2,1,0:T(8,128)(2,1)S(1)}, bf16[16,64,256]{2,1,0:T(8,128)(2,1)S(1)}, u32[]{:S(2)}, u32[]{:S(2)}) collective-permute-start(bf16[16,64,256]{2,1,0:T(8,128)(2,1)S(1)} %get-tuple-element.17), channel_id=1, source_target_pairs={{0,16},{8,24},{16,0},{24,8},{1,17},{9,25},{17,1},{25,9},{2,18},{10... | collective-permute-start | bytes 1572872 | tf_op jit(solution)/shard_map/ppermute | solution.py:13
  48.0 0.6 and_bitcast_fusion
  48.6 3.6 %copy.25 = pred[16,4,8,16,4,1]{3,0,4,5,2,1:T(8,128)(4,1)S(1)} copy(pred[16,4,8,16,4,1]{4,3,2,1,0,5:T(8,128)(4,1)S(1)} %and_bitcast_fusion) | data formatting | bytes 65536 | tf_op jit(solution)/shard_map/and | solution.py:24
  52.2 15.6 %collective-permute-done.7 = bf16[16,64,256]{2,1,0:T(8,128)(2,1)S(1)} collective-permute-done((bf16[16,64,256]{2,1,0:T(8,128)(2,1)S(1)}, bf16[16,64,256]{2,1,0:T(8,128)(2,1)S(1)}, u32[]{:S(2)}, u32[]{:S(2)}) %collective-permute-start.7) | collective-permute-done | bytes 524320 | tf_op jit(solution)/shard_map/ppermute | solution.py:13
  67.8 0.1 broadcast_select_fusion.1
  67.9 1.4 %reshape.120 = bf16[16,64,4,64,1,1]{3,2,1,0,4,5:T(4,128)(2,1)} reshape(bf16[16,64,256]{2,1,0:T(8,128)(2,1)S(1)} %broadcast_select_fusion.1) | data formatting | bytes 1048576 | tf_op jit(solution)/shard_map/while/body/eval_jaxpr/reshape | solution.py:25
  69.3 1.7 %collective-permute-start.11 = (bf16[16,64,256]{2,1,0:T(8,128)(2,1)S(1)}, bf16[16,64,256]{2,1,0:T(8,128)(2,1)S(1)}, u32[]{:S(2)}, u32[]{:S(2)}) collective-permute-start(bf16[16,64,256]{2,1,0:T(8,128)(2,1)S(1)} %broadcast_select_fusion.1), channel_id=1, source_target_pairs={{0,6},{2,0},{4,2},{6,4},{1,7},{3,1},{5,3},{7,5},{8,14},{10,8},{12,... | collective-permute-start | bytes 1572872 | tf_op jit(solution)/shard_map/while/body/eval_jaxpr/ppermute | solution.py:13
  71.0 0.0 collective-permute-done.1
  71.0 0.1 broadcast_select_fusion.3
  71.0 0.4 reshape.115
  71.4 0.8 collective-permute-start.8
  72.2 3.8 %fusion.6 = bf16[16,4,8,64,64,1]{4,0,5,3,2,1:T(8,128)(2,1)S(1)} fusion(pred[16,4,8,16,4,1]{3,0,4,5,2,1:T(8,128)(4,1)} %copy.20, bf16[16,64,4,64,1,1]{3,2,1,0,4,5:T(4,128)(2,1)} %reshape.120), kind=kOutput, calls=%fused_computation.11 | convolution fusion | flops 268435456 | bytes 4751360 | tf_op jit(solution)/shard_map/while/body/eval_jaxpr/rpokq,kbqc->rpobc/dot_general | solution.py:26
  76.0 6.7 %fusion = f32[16,64,8,64,1]{3,1,4,2,0:T(8,128)} fusion(bf16[16,4,8,64,64,1]{4,0,5,3,2,1:T(8,128)(2,1)S(1)} %fusion.6, bf16[16,64,4,64,1]{3,2,1,0,4:T(4,128)(2,1)S(1)} %bitcast.35), kind=kOutput, calls=%fused_computation.2 | convolution fusion | flops 268435456 | bytes 6815744 | tf_op jit(solution)/shard_map/while/body/eval_jaxpr/rapb,rpobc->raoc/dot_general | solution.py:29
  82.7 0.0 collective-permute-done.11
  82.7 0.4 reshape.125
  83.1 5.8 %fusion.4 = bf16[16,4,8,64,64,1]{4,0,5,3,2,1:T(8,128)(2,1)} fusion(pred[16,4,8,16,4,1]{3,0,4,5,2,1:T(8,128)(4,1)S(1)} %copy.25, bf16[16,64,4,64,1,1]{3,2,1,0,4,5:T(4,128)(2,1)S(1)} %reshape.125), kind=kOutput, calls=%fused_computation.9 | convolution fusion | flops 268435456 | bytes 4751360 | tf_op jit(solution)/shard_map/rpokq,kbqc->rpobc/dot_general | solution.py:26
  88.9 0.0 collective-permute-done.8
  88.9 2.0 %reshape.117 = bf16[16,64,4,64]{3,2,1,0:T(4,128)(2,1)S(1)} reshape(bf16[16,64,256]{2,1,0:T(8,128)(2,1)} %collective-permute-done.8) | data formatting | bytes 1048576 | tf_op jit(solution)/shard_map/reshape | solution.py:28
  90.9 9.4 %bitcast_add_fusion = f32[16,64,8,64]{3,1,2,0:T(8,128)S(1)} fusion(f32[16,64,8,64,1]{3,1,4,2,0:T(8,128)} %fusion, bf16[16,4,8,64,64,1]{4,0,5,3,2,1:T(8,128)(2,1)} %fusion.4, bf16[16,64,4,64,1]{3,2,1,0,4:T(4,128)(2,1)S(1)} %bitcast.34), kind=kOutput, calls=%fused_computation.4 | convolution fusion | flops 268959744 | bytes 8912896 | tf_op jit(solution)/shard_map/rapb,rpobc->raoc/dot_general | solution.py:29
  100.4 5.2 %copy.18 = f32[16,64,8,64]{3,2,1,0:T(8,128)} copy(f32[16,64,8,64]{3,1,2,0:T(8,128)S(1)} %bitcast_add_fusion) | data formatting | bytes 4194304 | tf_op jit(solution)/shard_map/add | solution.py:30
  105.6 4.8 %add.36 = f32[16,64,512]{2,1,0:T(8,128)} reshape(f32[16,64,8,64]{3,2,1,0:T(8,128)} %copy.18) | data formatting | bytes 4194304 | tf_op jit(solution)/shard_map/add | solution.py:30
  110.4 0.0 reduce-scatter.2.cloned.1.call-update
  110.4 10.4 %reduce-scatter.2.cloned.1.call-done = f32[16,64,256]{2,1,0:T(8,128)} async-done(((f32[16,64,512]{2,1,0:T(8,128)}), f32[16,64,256]{2,1,0:T(8,128)}) %reduce-scatter.2.cloned.1.call-update) | async-done | bytes 1048592 | tf_op jit(solution)/shard_map/reduce_scatter | solution.py:68
  120.8 3.3 %copy.19 = f32[16,64,1,256]{3,2,1,0:T(1,128)} copy(f32[16,64,1,256]{3,1,0,2:T(8,128)} %bitcast.36) | data formatting | bytes 2097152 | tf_op jit(solution)/shard_map/broadcast_in_dim | solution.py:69
  (3 shorter events, 0.0 us)
Async XLA Ops:
  6.5 114.2 %reduce-scatter.2.cloned.1.call-start = ((), (), s32[]{:S(2)}) async-start(), calls=%async_computation.1 | async-start | bytes 3145728 | tf_op jit(solution)/shard_map/reduce_scatter | solution.py:68
  8.4 35.9 %collective-permute-start = (bf16[16,64,256]{2,1,0:T(8,128)(2,1)S(1)}, bf16[16,64,256]{2,1,0:T(8,128)(2,1)S(1)}, u32[]{:S(2)}, u32[]{:S(2)}) collective-permute-start(bf16[16,64,256]{2,1,0:T(8,128)(2,1)S(1)} %bitcast_select_fusion), channel_id=1, source_target_pairs={{0,24},{8,0},{16,8},{24,16},{1,25},{9,1},{17,9},{25,17},{2,26},{10... | collective-permute-start | bytes 1572872 | tf_op jit(solution)/shard_map/ppermute | solution.py:13
  12.3 32.0 %collective-permute-start.6 = (bf16[16,64,256]{2,1,0:T(8,128)(2,1)S(1)}, bf16[16,64,256]{2,1,0:T(8,128)(2,1)S(1)}, u32[]{:S(2)}, u32[]{:S(2)}) collective-permute-start(bf16[16,64,256]{2,1,0:T(8,128)(2,1)S(1)} %bitcast_select_fusion), channel_id=1, source_target_pairs={{0,6},{2,0},{4,2},{6,4},{1,7},{3,1},{5,3},{7,5},{8,14},{10,8},{12,... | collective-permute-start | bytes 1572872 | tf_op jit(solution)/shard_map/ppermute | solution.py:13
  15.9 7.6 %collective-permute-start.2 = (s32[16,4]{0,1:T(4,128)}, s32[16,4]{0,1:T(4,128)S(1)}, u32[]{:S(2)}, u32[]{:S(2)}) collective-permute-start(s32[16,4]{0,1:T(4,128)} %bitcast.38), channel_id=1, source_target_pairs={{0,24},{8,0},{16,8},{24,16},{1,25},{9,1},{17,9},{25,17},{2,26},{10... | collective-permute-start | bytes 776 | tf_op jit(solution)/shard_map/ppermute | solution.py:13
  16.4 10.4 %collective-permute-start.4 = (s32[16,4]{0,1:T(4,128)}, s32[16,4]{0,1:T(4,128)S(1)}, u32[]{:S(2)}, u32[]{:S(2)}) collective-permute-start(s32[16,4]{0,1:T(4,128)} %bitcast.39), channel_id=1, source_target_pairs={{0,6},{2,0},{4,2},{6,4},{1,7},{3,1},{5,3},{7,5},{8,14},{10,8},{12,... | collective-permute-start | bytes 776 | tf_op jit(solution)/shard_map/ppermute | solution.py:13
  27.5 3.6 %collective-permute-start.3 = (s32[16,4]{0,1:T(4,128)S(1)}, s32[16,4]{0,1:T(4,128)S(1)}, u32[]{:S(2)}, u32[]{:S(2)}) collective-permute-start(s32[16,4]{0,1:T(4,128)S(1)} %get-tuple-element.28), channel_id=1, source_target_pairs={{0,16},{8,24},{16,0},{24,8},{1,17},{9,25},{17,1},{25,9},{2,18},{10... | collective-permute-start | bytes 776 | tf_op jit(solution)/shard_map/ppermute | solution.py:13
  28.8 4.5 %collective-permute-start.5 = (s32[16,4]{0,1:T(4,128)S(1)}, s32[16,4]{0,1:T(4,128)S(1)}, u32[]{:S(2)}, u32[]{:S(2)}) collective-permute-start(s32[16,4]{0,1:T(4,128)S(1)} %get-tuple-element.30), channel_id=1, source_target_pairs={{0,4},{2,6},{4,0},{6,2},{1,5},{3,7},{5,1},{7,3},{8,12},{10,14},{12... | collective-permute-start | bytes 776 | tf_op jit(solution)/shard_map/ppermute | solution.py:13
  31.2 13.0 %collective-permute-start.9 = (s32[16,4]{0,1:T(4,128)S(1)}, s32[16,4]{0,1:T(4,128)S(1)}, u32[]{:S(2)}, u32[]{:S(2)}) collective-permute-start(s32[16,4]{0,1:T(4,128)S(1)} %broadcast_select_fusion.7), channel_id=1, source_target_pairs={{0,24},{8,0},{16,8},{24,16},{1,25},{9,1},{17,9},{25,17},{2,26},{10... | collective-permute-start | bytes 776 | tf_op jit(solution)/shard_map/while/body/eval_jaxpr/ppermute | solution.py:13
  33.3 5.6 %collective-permute-start.10 = (s32[16,4]{0,1:T(4,128)S(1)}, s32[16,4]{0,1:T(4,128)S(1)}, u32[]{:S(2)}, u32[]{:S(2)}) collective-permute-start(s32[16,4]{0,1:T(4,128)S(1)} %broadcast_select_fusion.5), channel_id=1, source_target_pairs={{0,6},{2,0},{4,2},{6,4},{1,7},{3,1},{5,3},{7,5},{8,14},{10,8},{12,... | collective-permute-start | bytes 776 | tf_op jit(solution)/shard_map/while/body/eval_jaxpr/ppermute | solution.py:13
  45.4 22.4 %collective-permute-start.7 = (bf16[16,64,256]{2,1,0:T(8,128)(2,1)S(1)}, bf16[16,64,256]{2,1,0:T(8,128)(2,1)S(1)}, u32[]{:S(2)}, u32[]{:S(2)}) collective-permute-start(bf16[16,64,256]{2,1,0:T(8,128)(2,1)S(1)} %get-tuple-element.18), channel_id=1, source_target_pairs={{0,4},{2,6},{4,0},{6,2},{1,5},{3,7},{5,1},{7,3},{8,12},{10,14},{12... | collective-permute-start | bytes 1572872 | tf_op jit(solution)/shard_map/ppermute | solution.py:13
  46.4 24.6 %collective-permute-start.1 = (bf16[16,64,256]{2,1,0:T(8,128)(2,1)S(1)}, bf16[16,64,256]{2,1,0:T(8,128)(2,1)S(1)}, u32[]{:S(2)}, u32[]{:S(2)}) collective-permute-start(bf16[16,64,256]{2,1,0:T(8,128)(2,1)S(1)} %get-tuple-element.17), channel_id=1, source_target_pairs={{0,16},{8,24},{16,0},{24,8},{1,17},{9,25},{17,1},{25,9},{2,18},{10... | collective-permute-start | bytes 1572872 | tf_op jit(solution)/shard_map/ppermute | solution.py:13
  69.3 13.5 %collective-permute-start.11 = (bf16[16,64,256]{2,1,0:T(8,128)(2,1)S(1)}, bf16[16,64,256]{2,1,0:T(8,128)(2,1)S(1)}, u32[]{:S(2)}, u32[]{:S(2)}) collective-permute-start(bf16[16,64,256]{2,1,0:T(8,128)(2,1)S(1)} %broadcast_select_fusion.1), channel_id=1, source_target_pairs={{0,6},{2,0},{4,2},{6,4},{1,7},{3,1},{5,3},{7,5},{8,14},{10,8},{12,... | collective-permute-start | bytes 1572872 | tf_op jit(solution)/shard_map/while/body/eval_jaxpr/ppermute | solution.py:13
  71.4 17.5 %collective-permute-start.8 = (bf16[16,64,256]{2,1,0:T(8,128)(2,1)S(1)}, bf16[16,64,256]{2,1,0:T(8,128)(2,1)}, u32[]{:S(2)}, u32[]{:S(2)}) collective-permute-start(bf16[16,64,256]{2,1,0:T(8,128)(2,1)S(1)} %broadcast_select_fusion.3), channel_id=1, source_target_pairs={{0,24},{8,0},{16,8},{24,16},{1,25},{9,1},{17,9},{25,17},{2,26},{10... | collective-permute-start | bytes 1572872 | tf_op jit(solution)/shard_map/while/body/eval_jaxpr/ppermute | solution.py:13
Sparse Core Ops, SparseCore 0:
  110.5 10.1 reduce-scatter.1
where the time goes:
time: 131 us
  waiting for transfers between devices  39.5 us (30%)
  local copies, waits for them, and re-layouts  26.5 us (20%)
  matrix products  25.7 us (20%)
  starting transfers between devices  20.3 us (15%)
  between operations  13.5 us (10%)
  other arithmetic  5.51 us (4%)
    ppermute x12, waiting for transfers between devices, from_behind(): lax.ppermute(x, axis, [(i, (i + by) % devices) for i in range(devices)])  29.1 us
    ppermute x12, starting transfers between devices, from_behind(): lax.ppermute(x, axis, [(i, (i + by) % devices) for i in range(devices)])  20.3 us
    dot_general x2, matrix products, accumulate(): jnp.einsum('rapb,rpobc->raoc', factor, picked, preferred_element_type=jnp...  16.1 us
    reduce_scatter x1, waiting for transfers between devices, per_device(): share = lax.psum_scatter(total, 'layer', scatter_dimension=2, tiled=True)  10.4 us
    add x2, local copies, waits for them, and re-layouts, accumulate(): return total + result.reshape(row_count, width, -1)  10 us
    dot_general x2, matrix products, accumulate(): jnp.einsum('rpokq,kbqc->rpobc', select, blocks, preferred_element_type=jn...  9.6 us
    and x2, local copies, waits for them, and re-layouts, accumulate(): select = jnp.logical_and(take_row, take_slot).astype(jnp.bfloat16)  7.8 us
    broadcast_in_dim x1, local copies, waits for them, and re-layouts, per_device(): return share[:, :, None, :]  3.33 us
  transfers between devices with their start and end apart: 13, of which 7 were waited for; matrix products, arithmetic and copies ran while one was open for 23% of the time, Pallas kernels for 0%

commit v1 on v0

v1 whole, which is shorter than its diff:
```python
import jax
import jax.numpy as jnp
from jax import lax
from jax.sharding import PartitionSpec as P


def spread(values, cols, index_count):
    ids = lax.broadcasted_iota(jnp.int32, (1, index_count, 1), 1)
    hit = cols[:, None, :] == ids
    zero = jnp.zeros((), values.dtype)
    out = jnp.zeros(values.shape[:2] + (index_count, values.shape[3]), values.dtype)
    for s in range(values.shape[2]):
        out = out + jnp.where(hit[:, None, :, s, None], values[:, :, s, None, :], zero)
    return out


def per_device(x_blocks, x_cols, x_count, out_cols):
    row_count, width, _, lanes = x_blocks.shape
    slots = lanes // width
    values = x_blocks[:, :, 0, :]
    slot_of_lane = lax.broadcasted_iota(jnp.int32, (1, 1, lanes), 2) // width
    values = jnp.where(slot_of_lane < x_count[:, :, None], values, jnp.zeros((), values.dtype))
    columns = x_cols[:, 0, :]
    layers = lax.axis_size("layer")
    share = out_cols.shape[2] // layers
    wanted = lax.dynamic_slice_in_dim(out_cols[:, 0, :], lax.axis_index("layer") * share, share, axis=1)

    left_vals = lax.all_gather(values, "row")
    left_cols = lax.all_gather(columns, "row")
    upper_vals = lax.all_gather(values, "col")
    upper_cols = lax.all_gather(columns, "col")
    tiles = left_vals.shape[0]
    per_tile = row_count

    def step(t, total):
        a = left_vals[t].reshape(row_count, width, slots, width)
        a = spread(a, left_cols[t], per_tile)
        b = upper_vals[t].reshape(per_tile, width, slots, width)
        b = spread(b, upper_cols[t], per_tile)
        a = a.reshape(row_count * width, per_tile * width)
        b = b.reshape(per_tile * width, per_tile * width)
        return total + jnp.dot(a, b, preferred_element_type=jnp.float32)

    total = jnp.zeros((row_count * width, per_tile * width), jnp.float32)
    total = lax.fori_loop(0, tiles, step, total)
    total = total.reshape(row_count, width, per_tile, width)
    ids = lax.broadcasted_iota(jnp.int32, (1, 1, 1, per_tile, 1), 3)
    hit = wanted[:, None, :, None, None] == ids
    picked = jnp.where(hit, total[:, :, None, :, :], jnp.zeros((), jnp.float32)).sum(axis=3)
    return picked.reshape(row_count, width, 1, share * width)


def solution(mesh):
    placed = (
        P("col", None, "row", None),
        P("col", "row", None),
        P("col", "row"),
        P("col", "row", None),
    )
    return jax.shard_map(
        per_device,
        mesh=mesh,
        in_specs=placed,
        out_specs=P("col", None, "row", "layer"),
        check_vma=False,
    )
```

time: 131 us -> 267 us (2.04)
  local copies, waits for them, and re-layouts: 26.5 us -> 96.7 us
  other arithmetic: 5.51 us -> 42.7 us
  blocking collectives: 0 us -> 23 us
  waiting for transfers between devices: 39.5 us -> 61.5 us
  starting transfers between devices: 20.3 us -> 0.04 us
    all_gather x0 -> x2, waiting for transfers between devices: none -> 60.8 us  [the longest x1 47.5 us: per_device(): upper_vals = lax.all_gather(values, 'col')]
    add x2 -> x8, local copies, waits for them, and re-layouts: 10 us -> 48 us  [spread(): out + jnp.where(hit[:, None, :, s, None], values[:, :, s, None, :], zero)]
    ppermute x12 -> x0, waiting for transfers between devices: 29.1 us -> none  [from_behind(): lax.ppermute(x, axis, [(i, (i + by) % devices) for i in range(devices)])]
    add x0 -> x8, other arithmetic: none -> 27.6 us  [spread(): out + jnp.where(hit[:, None, :, s, None], values[:, :, s, None, :], zero)]
    all_gather x0 -> x2, blocking collectives: none -> 23 us  [the longest x1 13.4 us: per_device(): upper_cols = lax.all_gather(columns, 'col')]
    ppermute x12 -> x0, starting transfers between devices: 20.3 us -> none  [from_behind(): lax.ppermute(x, axis, [(i, (i + by) % devices) for i in range(devices)])]
    slice x0 -> x8, local copies, waits for them, and re-layouts: none -> 17.9 us  [spread(): values[:, :, s, None, :]]
    reduce_sum x0 -> x1, other arithmetic: none -> 11.8 us  [per_device(): jnp.where(hit, total[:, :, None, :, :], jnp.zeros((), jnp.float32))]
  transfers between devices with their start and end apart: 13 -> 2, of which waited for: 7 -> 2; matrix products, arithmetic and copies ran while one was open for 23% -> 0% of each run, Pallas kernels for 0% -> 0%
where the time goes in v1:
time: 267 us; the launch traced here: 265 us
  local copies, waits for them, and re-layouts  96.7 us (36%)
  waiting for transfers between devices  61.5 us (23%)
  other arithmetic  42.7 us (16%)
  matrix products  27.4 us (10%)
  blocking collectives  23 us (9%)
  between operations  13.4 us (5%)
    add x8, local copies, waits for them, and re-layouts, spread(): out + jnp.where(hit[:, None, :, s, None], values[:, :, s, None, :], zero)  48 us
    all_gather x1, waiting for transfers between devices, per_device(): upper_vals = lax.all_gather(values, 'col')  47.5 us
    add x8, other arithmetic, spread(): out + jnp.where(hit[:, None, :, s, None], values[:, :, s, None, :], zero)  27.6 us
    dot_general x4, matrix products, step(): return total + jnp.dot(a, b, preferred_element_type=jnp.float32)  27.4 us
    slice x8, local copies, waits for them, and re-layouts, spread(): values[:, :, s, None, :]  17.9 us
    all_gather x1, blocking collectives, per_device(): upper_cols = lax.all_gather(columns, 'col')  13.4 us
    all_gather x1, waiting for transfers between devices, per_device(): left_vals = lax.all_gather(values, 'row')  13.3 us
    reduce_sum x1, other arithmetic, per_device(): jnp.where(hit, total[:, :, None, :, :], jnp.zeros((), jnp.float32))  11.8 us
  transfers between devices with their start and end apart: 2, of which 2 were waited for; matrix products, arithmetic and copies ran while one was open for 0% of the time, Pallas kernels for 0%

profile of v1, /device:TPU:0, one launch (start us, length us, event | category | flops | bytes accessed | tf_op | source)
XLA Modules:
  0.0 265.3 jit_solution(14562152407944202302)
XLA Ops:
  6.5 0.7 broadcast_compare_fusion
  7.3 1.9 bitcast_select_fusion
  9.2 0.7 all-gather.7.cloned.1.call-update
  9.9 0.8 copy.21
  10.7 9.6 %all-gather = s32[64,1,4]{2,1,0:T(1,128)S(1)} all-gather(s32[16,1,4]{2,1,0:T(1,128)S(1)} %copy.21), channel_id=2, replica_groups=mesh['row'=4,'col'=4,'layer'=2] {'row'}, dimensions={0}, use_global_device_ids=true | all-gather | bytes 1280 | tf_op jit(solution)/shard_map/all_gather | solution.py:29
  20.3 0.1 copy.25
  20.4 13.4 %all-gather.1 = s32[64,1,4]{2,1,0:T(1,128)S(1)} all-gather(s32[16,1,4]{2,1,0:T(1,128)S(1)} %copy.21), channel_id=3, replica_groups=mesh['row'=4,'col'=4,'layer'=2] {'col'}, dimensions={0}, use_global_device_ids=true | all-gather | bytes 1280 | tf_op jit(solution)/shard_map/all_gather | solution.py:31
  33.8 0.1 copy.26
  33.9 0.1 copy.20
  34.0 0.1 iota_compare_fusion.2
  34.1 13.3 %all-gather.5.cloned.1.call-done = bf16[4,16,64,256]{3,2,1,0:T(8,128)(2,1)} async-done(((bf16[1,16,64,256]{3,2,1,0:T(8,128)(2,1)}), bf16[4,16,64,256]{3,2,1,0:T(8,128)(2,1)}) %all-gather.5.cloned.1.call-update) | async-done | bytes 2097168 | tf_op jit(solution)/shard_map/all_gather | solution.py:28
  47.4 47.5 %all-gather.7.cloned.1.call-done = bf16[4,16,64,256]{3,2,1,0:T(8,128)(2,1)} async-done(((bf16[1,16,64,256]{3,2,1,0:T(8,128)(2,1)}), bf16[4,16,64,256]{3,2,1,0:T(8,128)(2,1)}) %all-gather.7.cloned.1.call-update) | async-done | bytes 2097168 | tf_op jit(solution)/shard_map/all_gather | solution.py:30
  94.9 141.5 %while.14 = (s32[]{:T(128)}, f32[1024,1024]{1,0:T(8,128)}, s32[4,16,4]{1,2,0:T(4,128)S(1)}, bf16[4,16,64,256]{3,2,1,0:T(8,128)(2,1)}, s32[4,16,4]{1,2,0:T(4,128)...) while((s32[]{:T(128)}, f32[1024,1024]{1,0:T(8,128)}, ...), condition=%wide.region_1.2_spmd.clone, body=%wide.region_0.1_spmd.clone.sunk | while | flops 2164262912 | bytes 34612844 | solution.py:45
  94.9 0.1 iota_compare_fusion.5
  95.0 2.1 constant_dynamic-slice_fusion.3
  97.1 0.4 squeeze.53
  97.5 2.2 fusion.10
  99.9 3.5 %select_add_fusion.6 = bf16[16,64,16,64]{3,2,1,0:T(8,128)(2,1)} fusion(pred[16,16]{1,0:T(8,128)(4,1)S(1)} %get-tuple-element.250, pred[16,16]{1,0:T(8,128)(4,1)S(1)} %get-tuple-element.251, pred[16,16]{1,0:T(8,128)(4,1)S(1)} %get-tuple-element.252, pred[16,16]{1,0:T(8,128)(4,1)S(1)} %get-tuple-element.253, bf16[16,64,64]{2,1,0:T(8,128)(2,1)S(1)} %bitcast.87, ...), kind=kLoop, calls=%fused_computation.2.clone.1 | loop fusion | flops 7340032 | bytes 2622464 | tf_op jit(solution)/shard_map/while/body/eval_jaxpr/add | solution.py:13
  103.4 5.5 %add.170 = bf16[1024,1024]{1,0:T(8,128)(2,1)S(1)} reshape(bf16[16,64,16,64]{3,2,1,0:T(8,128)(2,1)} %select_add_fusion.6) | data formatting | bytes 4194304 | tf_op jit(solution)/shard_map/while/body/eval_jaxpr/add | solution.py:13
  108.9 0.1 iota_compare_fusion.6
  109.0 2.0 squeeze.54
  111.0 2.2 fusion.11
  113.4 3.5 %select_add_fusion.7 = bf16[16,64,16,64]{3,2,1,0:T(8,128)(2,1)} fusion(pred[16,16]{1,0:T(8,128)(4,1)S(1)} %get-tuple-element.260, pred[16,16]{1,0:T(8,128)(4,1)S(1)} %get-tuple-element.261, pred[16,16]{1,0:T(8,128)(4,1)S(1)} %get-tuple-element.262, pred[16,16]{1,0:T(8,128)(4,1)S(1)} %get-tuple-element.263, bf16[16,64,64]{2,1,0:T(8,128)(2,1)S(1)} %bitcast.88, ...), kind=kLoop, calls=%fused_computation.1.clone.1 | loop fusion | flops 7340032 | bytes 2622464 | tf_op jit(solution)/shard_map/while/body/eval_jaxpr/add | solution.py:13
  116.9 6.5 %add.171 = bf16[1024,1024]{1,0:T(8,128)(2,1)} reshape(bf16[16,64,16,64]{3,2,1,0:T(8,128)(2,1)} %select_add_fusion.7) | data formatting | bytes 4194304 | tf_op jit(solution)/shard_map/while/body/eval_jaxpr/add | solution.py:13
  123.4 5.9 %select_add_fusion.8 = f32[1024,1024]{1,0:T(8,128)} fusion(f32[1024,1024]{1,0:T(8,128)} %get-tuple-element.278, pred[]{:T(512)S(6)} %compare.9, bf16[1024,1024]{1,0:T(8,128)(2,1)S(1)} %add.170, bf16[1024,1024]{1,0:T(8,128)(2,1)} %add.171), kind=kOutput, calls=%fused_computation.clone.1 | convolution fusion | flops 2149580800 | bytes 12582913 | tf_op jit(solution)/shard_map/while/body/eval_jaxpr/dot_general | solution.py:42
  129.3 0.1 iota_compare_fusion.5
  129.4 2.1 constant_dynamic-slice_fusion.3
  131.5 0.4 squeeze.53
  132.0 2.2 fusion.10
  134.4 3.5 %select_add_fusion.6 = bf16[16,64,16,64]{3,2,1,0:T(8,128)(2,1)} fusion(pred[16,16]{1,0:T(8,128)(4,1)S(1)} %get-tuple-element.250, pred[16,16]{1,0:T(8,128)(4,1)S(1)} %get-tuple-element.251, pred[16,16]{1,0:T(8,128)(4,1)S(1)} %get-tuple-element.252, pred[16,16]{1,0:T(8,128)(4,1)S(1)} %get-tuple-element.253, bf16[16,64,64]{2,1,0:T(8,128)(2,1)S(1)} %bitcast.87, ...), kind=kLoop, calls=%fused_computation.2.clone.1 | loop fusion | flops 7340032 | bytes 2622464 | tf_op jit(solution)/shard_map/while/body/eval_jaxpr/add | solution.py:13
  137.8 5.5 %add.170 = bf16[1024,1024]{1,0:T(8,128)(2,1)S(1)} reshape(bf16[16,64,16,64]{3,2,1,0:T(8,128)(2,1)} %select_add_fusion.6) | data formatting | bytes 4194304 | tf_op jit(solution)/shard_map/while/body/eval_jaxpr/add | solution.py:13
  143.3 0.1 iota_compare_fusion.6
  143.4 2.0 squeeze.54
  145.5 2.2 fusion.11
  147.9 3.5 %select_add_fusion.7 = bf16[16,64,16,64]{3,2,1,0:T(8,128)(2,1)} fusion(pred[16,16]{1,0:T(8,128)(4,1)S(1)} %get-tuple-element.260, pred[16,16]{1,0:T(8,128)(4,1)S(1)} %get-tuple-element.261, pred[16,16]{1,0:T(8,128)(4,1)S(1)} %get-tuple-element.262, pred[16,16]{1,0:T(8,128)(4,1)S(1)} %get-tuple-element.263, bf16[16,64,64]{2,1,0:T(8,128)(2,1)S(1)} %bitcast.88, ...), kind=kLoop, calls=%fused_computation.1.clone.1 | loop fusion | flops 7340032 | bytes 2622464 | tf_op jit(solution)/shard_map/while/body/eval_jaxpr/add | solution.py:13
  151.3 6.5 %add.171 = bf16[1024,1024]{1,0:T(8,128)(2,1)} reshape(bf16[16,64,16,64]{3,2,1,0:T(8,128)(2,1)} %select_add_fusion.7) | data formatting | bytes 4194304 | tf_op jit(solution)/shard_map/while/body/eval_jaxpr/add | solution.py:13
  157.9 7.2 %select_add_fusion.8 = f32[1024,1024]{1,0:T(8,128)} fusion(f32[1024,1024]{1,0:T(8,128)} %get-tuple-element.278, pred[]{:T(512)S(6)} %compare.9, bf16[1024,1024]{1,0:T(8,128)(2,1)S(1)} %add.170, bf16[1024,1024]{1,0:T(8,128)(2,1)} %add.171), kind=kOutput, calls=%fused_computation.clone.1 | convolution fusion | flops 2149580800 | bytes 12582913 | tf_op jit(solution)/shard_map/while/body/eval_jaxpr/dot_general | solution.py:42
  165.0 0.1 iota_compare_fusion.5
  165.1 2.1 constant_dynamic-slice_fusion.3
  167.2 0.4 squeeze.53
  167.6 2.2 fusion.10
  170.1 3.5 %select_add_fusion.6 = bf16[16,64,16,64]{3,2,1,0:T(8,128)(2,1)} fusion(pred[16,16]{1,0:T(8,128)(4,1)S(1)} %get-tuple-element.250, pred[16,16]{1,0:T(8,128)(4,1)S(1)} %get-tuple-element.251, pred[16,16]{1,0:T(8,128)(4,1)S(1)} %get-tuple-element.252, pred[16,16]{1,0:T(8,128)(4,1)S(1)} %get-tuple-element.253, bf16[16,64,64]{2,1,0:T(8,128)(2,1)S(1)} %bitcast.87, ...), kind=kLoop, calls=%fused_computation.2.clone.1 | loop fusion | flops 7340032 | bytes 2622464 | tf_op jit(solution)/shard_map/while/body/eval_jaxpr/add | solution.py:13
  173.5 5.5 %add.170 = bf16[1024,1024]{1,0:T(8,128)(2,1)S(1)} reshape(bf16[16,64,16,64]{3,2,1,0:T(8,128)(2,1)} %select_add_fusion.6) | data formatting | bytes 4194304 | tf_op jit(solution)/shard_map/while/body/eval_jaxpr/add | solution.py:13
  179.0 0.1 iota_compare_fusion.6
  179.1 2.0 squeeze.54
  181.1 2.2 fusion.11
  183.6 3.5 %select_add_fusion.7 = bf16[16,64,16,64]{3,2,1,0:T(8,128)(2,1)} fusion(pred[16,16]{1,0:T(8,128)(4,1)S(1)} %get-tuple-element.260, pred[16,16]{1,0:T(8,128)(4,1)S(1)} %get-tuple-element.261, pred[16,16]{1,0:T(8,128)(4,1)S(1)} %get-tuple-element.262, pred[16,16]{1,0:T(8,128)(4,1)S(1)} %get-tuple-element.263, bf16[16,64,64]{2,1,0:T(8,128)(2,1)S(1)} %bitcast.88, ...), kind=kLoop, calls=%fused_computation.1.clone.1 | loop fusion | flops 7340032 | bytes 2622464 | tf_op jit(solution)/shard_map/while/body/eval_jaxpr/add | solution.py:13
  187.0 6.5 %add.171 = bf16[1024,1024]{1,0:T(8,128)(2,1)} reshape(bf16[16,64,16,64]{3,2,1,0:T(8,128)(2,1)} %select_add_fusion.7) | data formatting | bytes 4194304 | tf_op jit(solution)/shard_map/while/body/eval_jaxpr/add | solution.py:13
  193.6 7.2 %select_add_fusion.8 = f32[1024,1024]{1,0:T(8,128)} fusion(f32[1024,1024]{1,0:T(8,128)} %get-tuple-element.278, pred[]{:T(512)S(6)} %compare.9, bf16[1024,1024]{1,0:T(8,128)(2,1)S(1)} %add.170, bf16[1024,1024]{1,0:T(8,128)(2,1)} %add.171), kind=kOutput, calls=%fused_computation.clone.1 | convolution fusion | flops 2149580800 | bytes 12582913 | tf_op jit(solution)/shard_map/while/body/eval_jaxpr/dot_general | solution.py:42
  200.7 0.1 iota_compare_fusion.5
  200.8 2.1 constant_dynamic-slice_fusion.3
  202.9 0.4 squeeze.53
  203.3 2.2 fusion.10
  205.8 3.5 %select_add_fusion.6 = bf16[16,64,16,64]{3,2,1,0:T(8,128)(2,1)} fusion(pred[16,16]{1,0:T(8,128)(4,1)S(1)} %get-tuple-element.250, pred[16,16]{1,0:T(8,128)(4,1)S(1)} %get-tuple-element.251, pred[16,16]{1,0:T(8,128)(4,1)S(1)} %get-tuple-element.252, pred[16,16]{1,0:T(8,128)(4,1)S(1)} %get-tuple-element.253, bf16[16,64,64]{2,1,0:T(8,128)(2,1)S(1)} %bitcast.87, ...), kind=kLoop, calls=%fused_computation.2.clone.1 | loop fusion | flops 7340032 | bytes 2622464 | tf_op jit(solution)/shard_map/while/body/eval_jaxpr/add | solution.py:13
  209.2 5.5 %add.170 = bf16[1024,1024]{1,0:T(8,128)(2,1)S(1)} reshape(bf16[16,64,16,64]{3,2,1,0:T(8,128)(2,1)} %select_add_fusion.6) | data formatting | bytes 4194304 | tf_op jit(solution)/shard_map/while/body/eval_jaxpr/add | solution.py:13
  214.7 0.1 iota_compare_fusion.6
  214.8 2.0 squeeze.54
  216.8 2.2 fusion.11
  219.3 3.5 %select_add_fusion.7 = bf16[16,64,16,64]{3,2,1,0:T(8,128)(2,1)} fusion(pred[16,16]{1,0:T(8,128)(4,1)S(1)} %get-tuple-element.260, pred[16,16]{1,0:T(8,128)(4,1)S(1)} %get-tuple-element.261, pred[16,16]{1,0:T(8,128)(4,1)S(1)} %get-tuple-element.262, pred[16,16]{1,0:T(8,128)(4,1)S(1)} %get-tuple-element.263, bf16[16,64,64]{2,1,0:T(8,128)(2,1)S(1)} %bitcast.88, ...), kind=kLoop, calls=%fused_computation.1.clone.1 | loop fusion | flops 7340032 | bytes 2622464 | tf_op jit(solution)/shard_map/while/body/eval_jaxpr/add | solution.py:13
  222.7 6.5 %add.171 = bf16[1024,1024]{1,0:T(8,128)(2,1)} reshape(bf16[16,64,16,64]{3,2,1,0:T(8,128)(2,1)} %select_add_fusion.7) | data formatting | bytes 4194304 | tf_op jit(solution)/shard_map/while/body/eval_jaxpr/add | solution.py:13
  229.3 7.2 %select_add_fusion.8 = f32[1024,1024]{1,0:T(8,128)} fusion(f32[1024,1024]{1,0:T(8,128)} %get-tuple-element.278, pred[]{:T(512)S(6)} %compare.9, bf16[1024,1024]{1,0:T(8,128)(2,1)S(1)} %add.170, bf16[1024,1024]{1,0:T(8,128)(2,1)} %add.171), kind=kOutput, calls=%fused_computation.clone.1 | convolution fusion | flops 2149580800 | bytes 12582913 | tf_op jit(solution)/shard_map/while/body/eval_jaxpr/dot_general | solution.py:42
  236.4 7.3 %broadcast_in_dim.302 = f32[16,64,16,64]{3,2,1,0:T(8,128)} reshape(f32[1024,1024]{1,0:T(8,128)} %get-tuple-element.114) | data formatting | bytes 8388608 | tf_op jit(solution)/shard_map/jit(_where)/broadcast_in_dim | solution.py:49
  243.7 11.8 %select_reduce_fusion = f32[16,64,4,64]{3,2,1,0:T(4,128)S(1)} fusion(f32[16,64,16,64]{3,2,1,0:T(8,128)} %broadcast_in_dim.302, pred[16,4,16]{2,1,0:T(4,128)(4,1)S(1)} %iota_compare_fusion.2), kind=kLoop, calls=%fused_computation.25 | loop fusion | flops 8126464 | bytes 5243904 | tf_op jit(solution)/shard_map/reduce_sum | solution.py:49
  255.5 2.9 %reshape.187 = f32[16,64,1,256]{3,2,1,0:T(1,128)} reshape(f32[16,64,4,64]{3,2,1,0:T(4,128)S(1)} %select_reduce_fusion) | data formatting | bytes 2097152 | tf_op jit(solution)/shard_map/reshape | solution.py:50
  (52 shorter events, 1.4 us)
Async XLA Ops:
  6.5 27.3 %copy-start = (s32[16,1,8]{0,2,1:T(8,128)S(1)}, s32[16,1,8]{0,2,1:T(8,128)}, u32[]{:S(2)}) copy-start(s32[16,1,8]{0,2,1:T(8,128)} %param.9) | copy-start | bytes 1540
  6.5 40.8 %all-gather.5.cloned.1.call-start = ((), (), s32[]{:S(2)}) async-start(), calls=%async_computation | async-start | bytes 2621440 | tf_op jit(solution)/shard_map/all_gather | solution.py:28
  9.2 85.7 %all-gather.7.cloned.1.call-start = ((), (), s32[]{:S(2)}) async-start(), calls=%async_computation.1 | async-start | bytes 2621440 | tf_op jit(solution)/shard_map/all_gather | solution.py:30
Sparse Core Ops, SparseCore 0:
  9.3 38.0 all-gather.4
  48.9 45.9 all-gather.6

commit v2 on v1

v2 whole, which is shorter than its diff:
```python
import functools

import jax
import jax.numpy as jnp
from jax import lax
from jax.experimental import pallas as pl
from jax.experimental.pallas import tpu as pltpu
from jax.sharding import PartitionSpec as P


def step_kernel(a_cols, b_cols, want, a_ref, b_ref, acc_ref, out_ref, big_ref):
    width = a_ref.shape[1]
    slots = a_ref.shape[2] // width
    outs = want.shape[0] // pl.num_programs(0)
    seg = slots * width
    r = pl.program_id(0)
    chunk = lax.broadcasted_iota(jnp.int32, (width, seg), 1) // width
    zero = jnp.zeros((width, seg), b_ref.dtype)
    for p in range(slots):
        k = a_cols[r * slots + p]
        blk = b_ref[k]
        for o in range(outs):
            j = want[r * outs + o]
            hit = jnp.int32(slots)
            for q in range(slots):
                hit = jnp.where(b_cols[k * slots + q] == j, jnp.int32(q), hit)
            big_ref[p * width:(p + 1) * width, o * seg:(o + 1) * seg] = jnp.where(chunk == hit, blk, zero)
    prod = jnp.dot(a_ref[0], big_ref[...], preferred_element_type=jnp.float32)
    lane = lax.broadcasted_iota(jnp.int32, (width, 2 * width), 1)
    groups = []
    folded = []
    for o in range(outs):
        part = prod[:, o * seg:(o + 1) * seg]
        half = seg // 2
        while half >= width:
            part = part + pltpu.roll(part, half, 1)
            half //= 2
        folded.append(part[:, :2 * width])
    for g in range(outs // 2):
        groups.append(jnp.where(lane < width, folded[2 * g], folded[2 * g + 1]))
    out_ref[0] = acc_ref[0] + jnp.concatenate(groups, axis=1)


def one_step(acc, left, right, a_cols, b_cols, want):
    rows, width, seg = acc.shape[0], left.shape[1], left.shape[2]
    outs = want.shape[0] // rows
    grid_spec = pltpu.PrefetchScalarGridSpec(
        num_scalar_prefetch=3,
        grid=(rows,),
        in_specs=[
            pl.BlockSpec((1, width, seg), lambda r, *_: (r, 0, 0)),
            pl.BlockSpec(right.shape, lambda r, *_: (0, 0, 0)),
            pl.BlockSpec((1, width, acc.shape[2]), lambda r, *_: (r, 0, 0)),
        ],
        out_specs=pl.BlockSpec((1, width, acc.shape[2]), lambda r, *_: (r, 0, 0)),
        scratch_shapes=[pltpu.VMEM((seg, outs * seg), right.dtype)],
    )
    return pl.pallas_call(
        step_kernel,
        grid_spec=grid_spec,
        out_shape=jax.ShapeDtypeStruct(acc.shape, acc.dtype),
        input_output_aliases={5: 0},
    )(a_cols, b_cols, want, left, right, acc)


def per_device(x_blocks, x_cols, x_count, out_cols):
    row_count, width, _, lanes = x_blocks.shape
    slots = lanes // width
    values = x_blocks[:, :, 0, :]
    slot_of_lane = lax.broadcasted_iota(jnp.int32, (1, 1, lanes), 2) // width
    values = jnp.where(slot_of_lane < x_count[:, :, None], values, jnp.zeros((), values.dtype))
    columns = x_cols[:, 0, :].reshape(-1)
    extra = jnp.zeros((1, width, lanes), values.dtype)
    extra = extra.at[0, 0, :columns.shape[0]].set(columns.astype(values.dtype))
    payload = jnp.concatenate([values, extra], axis=0)

    rows_n = lax.axis_size("row")
    cols_n = lax.axis_size("col")
    layers = lax.axis_size("layer")
    steps = rows_n // layers
    me_r = lax.axis_index("row")
    me_c = lax.axis_index("col")
    me_l = lax.axis_index("layer")

    def flat(r, c, l):
        return (r * cols_n + c) * layers + l

    want = out_cols[:, 0, :].reshape(-1)
    outs = out_cols.shape[2]
    total = jnp.zeros((row_count, width, outs * width), jnp.float32)
    for s in range(steps):
        left_pairs = []
        right_pairs = []
        for r in range(rows_n):
            for c in range(cols_n):
                for l in range(layers):
                    t = (r + c + s + l * steps) % rows_n
                    left_pairs.append((flat(t, c, l), flat(r, c, l)))
                    right_pairs.append((flat(r, t, l), flat(r, c, l)))
        left = lax.ppermute(payload, ("row", "col", "layer"), left_pairs)
        right = lax.ppermute(payload, ("row", "col", "layer"), right_pairs)
        a_cols = left[row_count, 0, :columns.shape[0]].astype(jnp.int32)
        b_cols = right[row_count, 0, :columns.shape[0]].astype(jnp.int32)
        total = one_step(total, left, right, a_cols, b_cols, want)

    share = outs // layers * width
    if layers == 2:
        mine = lax.dynamic_slice_in_dim(total, me_l * share, share, axis=2)
        theirs = lax.dynamic_slice_in_dim(total, (1 - me_l) * share, share, axis=2)
        got = lax.ppermute(theirs, "layer", [(0, 1), (1, 0)])
        result = mine + got
    else:
        result = lax.psum_scatter(total, "layer", scatter_dimension=2, tiled=True)
    return result[:, :, None, :]


def solution(mesh):
    placed = (
        P("col", None, "row", None),
        P("col", "row", None),
        P("col", "row"),
        P("col", "row", None),
    )
    return jax.shard_map(
        per_device,
        mesh=mesh,
        in_specs=placed,
        out_specs=P("col", None, "row", "layer"),
        check_vma=False,
    )
```

time: 267 us -> 71.7 us (0.27)
  local copies, waits for them, and re-layouts: 96.7 us -> 6.04 us
  waiting for transfers between devices: 61.5 us -> 16.7 us
  other arithmetic: 42.7 us -> 6.29 us
  matrix products: 27.4 us -> 0 us
  Pallas kernels: 0 us -> 26.8 us
  blocking collectives: 23 us -> 0 us
  starting transfers between devices: 0.04 us -> 14.7 us
  between operations: 13.4 us -> 0.1 us
    all_gather x2 -> x0, waiting for transfers between devices: 60.8 us -> none  [the longest x1 47.5 us: per_device(): upper_vals = lax.all_gather(values, 'col')]
    add x8 -> x0, local copies, waits for them, and re-layouts: 48 us -> none  [spread(): out + jnp.where(hit[:, None, :, s, None], values[:, :, s, None, :], zero)]
    add x8 -> x0, other arithmetic: 27.6 us -> none  [spread(): out + jnp.where(hit[:, None, :, s, None], values[:, :, s, None, :], zero)]
    dot_general x4 -> x0, matrix products: 27.4 us -> none  [step(): return total + jnp.dot(a, b, preferred_element_type=jnp.float32)]
    pallas_call x0 -> x2, Pallas kernels: none -> 26.8 us  [one_step(): pl.pallas_call(step_kernel, grid_spec=grid_spec, out_shape=jax.ShapeDtype...]
    all_gather x2 -> x0, blocking collectives: 23 us -> none  [the longest x1 13.4 us: per_device(): upper_cols = lax.all_gather(columns, 'col')]
    slice x8 -> x0, local copies, waits for them, and re-layouts: 17.9 us -> none  [spread(): values[:, :, s, None, :]]
    ppermute x0 -> x5, waiting for transfers between devices: none -> 16.7 us  [the longest x2 13.9 us: per_device(): right = lax.ppermute(payload, ('row', 'col', 'layer'), right_pairs)]
  transfers between devices with their start and end apart: 2 -> 5, of which waited for: 2 -> 2; matrix products, arithmetic and copies ran while one was open for 0% -> 3% of each run, Pallas kernels for 0% -> 0%
where the time goes in v2:
time: 71.7 us; the launch traced here: 70.6 us
  Pallas kernels  26.8 us (37%)
  waiting for transfers between devices  16.7 us (23%)
  starting transfers between devices  14.7 us (21%)
  other arithmetic  6.29 us (9%)
  local copies, waits for them, and re-layouts  6.04 us (8%)
    pallas_call x2, Pallas kernels, one_step(): pl.pallas_call(step_kernel, grid_spec=grid_spec, out_shape=jax.ShapeDtype...  26.8 us
    ppermute x2, waiting for transfers between devices, per_device(): right = lax.ppermute(payload, ('row', 'col', 'layer'), right_pairs)  13.9 us
    ppermute x2, starting transfers between devices, per_device(): right = lax.ppermute(payload, ('row', 'col', 'layer'), right_pairs)  12 us
    ppermute x1, waiting for transfers between devices, per_device(): got = lax.ppermute(theirs, 'layer', [(0, 1), (1, 0)])  2.77 us
    ppermute x2, starting transfers between devices, per_device(): left = lax.ppermute(payload, ('row', 'col', 'layer'), left_pairs)  2.62 us
    broadcast_in_dim x1, local copies, waits for them, and re-layouts, per_device(): return result[:, :, None, :]  2.05 us
    broadcast_in_dim x1, local copies, waits for them, and re-layouts, per_device(): total = jnp.zeros((row_count, width, outs * width), jnp.float32)  1.6 us
    dynamic_slice x1, local copies, waits for them, and re-layouts, per_device(): theirs = lax.dynamic_slice_in_dim(total, (1 - me_l) * share, share, axis=2)  1.47 us
  transfers between devices with their start and end apart: 5, of which 2 were waited for; matrix products, arithmetic and copies ran while one was open for 3% of the time, Pallas kernels for 0%

profile of v2, /device:TPU:0, one launch (start us, length us, event | category | flops | bytes accessed | tf_op | source)
XLA Modules:
  0.0 70.6 jit_solution(17502207656234651533)
XLA Ops:
  0.0 0.0 copy-start.5
  0.0 0.7 convert_element_type.31
  0.7 0.1 copy.10
  0.8 0.1 convert_element_type.32
  0.9 0.7 %broadcast_compare_fusion = pred[16,256]{1,0:T(8,128)(4,1)S(1)} fusion(s32[256]{0:T(256)S(1)} %and_select_fusion, s32[16]{0:T(128)} %bitcast.29), kind=kLoop, calls=%fused_computation.5 | loop fusion | flops 4096 | bytes 5184 | tf_op jit(solution)/shard_map/lt | solution.py:71
  1.6 1.1 %bitcast_select_fusion = bf16[16,64,256]{2,1,0:T(8,128)(2,1)S(1)} fusion(bf16[16,64,1,256]{3,1,2,0:T(8,128)(2,1)} %param.6, pred[16,256]{1,0:T(8,128)(4,1)S(1)} %broadcast_compare_fusion), kind=kLoop, calls=%fused_computation.4 | loop fusion | flops 262144 | bytes 1052672 | tf_op jit(solution)/shard_map/jit(_where)/select_n | solution.py:71
  2.8 0.7 collective-permute-start.3
  3.5 0.7 collective-permute-start.2
  4.2 11.3 %collective-permute-start.1 = (bf16[17,64,256]{2,1,0:T(8,128)(2,1)S(1)}, bf16[17,64,256]{2,1,0:T(8,128)(2,1)S(1)}, u32[]{:S(2)}, u32[]{:S(2)}) collective-permute-start(bf16[17,64,256]{2,1,0:T(8,128)(2,1)S(1)} %fusion.1), channel_id=1, source_target_pairs={{2,0},{7,1},{4,2},{1,3},{6,4},{3,5},{0,6},{5,7},{12,8},{9,9},{14,1... | collective-permute-start | bytes 1671176 | tf_op jit(solution)/shard_map/ppermute | solution.py:101
  15.5 1.9 %collective-permute-start = (bf16[17,64,256]{2,1,0:T(8,128)(2,1)S(1)}, bf16[17,64,256]{2,1,0:T(8,128)(2,1)S(1)}, u32[]{:S(2)}, u32[]{:S(2)}) collective-permute-start(bf16[17,64,256]{2,1,0:T(8,128)(2,1)S(1)} %fusion.1), channel_id=1, source_target_pairs={{8,0},{25,1},{18,2},{3,3},{28,4},{13,5},{6,6},{23,7},{16,8},{1,9},... | collective-permute-start | bytes 1671176 | tf_op jit(solution)/shard_map/ppermute | solution.py:100
  17.4 0.0 copy-done.5
  17.4 0.1 copy.11
  17.5 0.6 reshape_squeeze.4.want
  18.2 0.0 collective-permute-done.3.b_ref
  18.2 0.0 copy-start.1
  18.2 0.6 fusion.2.b_cols
  18.8 0.0 collective-permute-done.2.a_ref
  18.8 0.0 copy-start.3
  18.8 0.6 fusion.3.a_cols
  19.3 13.9 %collective-permute-done.1.b_ref = bf16[17,64,256]{2,1,0:T(8,128)(2,1)S(1)} collective-permute-done((bf16[17,64,256]{2,1,0:T(8,128)(2,1)S(1)}, bf16[17,64,256]{2,1,0:T(8,128)(2,1)S(1)}, u32[]{:S(2)}, u32[]{:S(2)}) %collective-permute-start.1) | collective-permute-done | bytes 557088 | tf_op jit(solution)/shard_map/ppermute | solution.py:101
  33.3 0.0 copy-start.2
  33.3 0.6 fusion.4.b_cols
  33.8 0.0 collective-permute-done.a_ref
  33.8 0.0 copy-start.4
  33.8 0.6 fusion.5.a_cols
  34.4 1.6 %broadcast_in_dim.22.acc_ref = f32[16,64,512]{2,1,0:T(8,128)} broadcast(f32[]{:T(128)} %constant.57.clone.1), dimensions={} | broadcast | bytes 2097156 | tf_op jit(solution)/shard_map/broadcast_in_dim | solution.py:90
  36.0 0.0 copy-done.1
  36.0 0.0 copy-done.3
  36.0 13.4 %shard_map.46.acc_ref = f32[16,64,512]{2,1,0:T(8,128)} custom-call(s32[64]{0:T(128)} %fusion.3.a_cols, s32[64]{0:T(128)} %fusion.2.b_cols, s32[128]{0:T(128)} %reshape_squeeze.4.want, bf16[17,64,256]{2,1,0:T(8,128)(2,1)} %copy-done.3, bf16[17,64,256]{2,1,0:T(8,128)(2,1)} %copy-done.1, ...), custom_call_target="tpu_custom_call", output_to_operand_aliasing={{}: (5, {})} | custom-call | tf_op jit(solution)/shard_map/pallas_call | solution.py:58
  49.4 0.0 copy-done.2
  49.4 0.0 copy-done.4
  49.4 13.4 %shard_map.47 = f32[16,64,512]{2,1,0:T(8,128)} custom-call(s32[64]{0:T(128)} %fusion.5.a_cols, s32[64]{0:T(128)} %fusion.4.b_cols, s32[128]{0:T(128)} %reshape_squeeze.4.want, bf16[17,64,256]{2,1,0:T(8,128)(2,1)} %copy-done.4, bf16[17,64,256]{2,1,0:T(8,128)(2,1)} %copy-done.2, f32[16,64,512]{2,1,0:T(8,128)} %shard_map.46.acc_ref), custom_call_target="tpu_custom_call", output_to_operand_aliasing={{}: (5, {})} | custom-call | tf_op jit(solution)/shard_map/pallas_call | solution.py:58
  62.8 0.0 copy-start
  62.8 1.5 %constant_dynamic-slice_fusion = f32[16,64,256]{2,1,0:T(8,128)S(1)} fusion(f32[16,64,512]{2,1,0:T(8,128)} %shard_map.47, s32[]{:T(128)S(6)} %select_n.23), kind=kLoop, calls=%fused_computation.18 | loop fusion | bytes 2097156 | tf_op jit(solution)/shard_map/dynamic_slice | solution.py:109
  64.3 0.1 collective-permute-start.4
  64.4 2.8 %collective-permute-done.4 = f32[16,64,256]{2,1,0:T(8,128)} collective-permute-done((f32[16,64,256]{2,1,0:T(8,128)S(1)}, f32[16,64,256]{2,1,0:T(8,128)}, u32[]{:S(2)}, u32[]{:S(2)}) %collective-permute-start.4) | collective-permute-done | bytes 1048608 | tf_op jit(solution)/shard_map/ppermute | solution.py:110
  67.2 0.0 copy-done
  67.2 1.4 %add_bitcast_fusion = f32[16,64,1,256]{3,1,0,2:T(8,128)S(1)} fusion(f32[16,64,256]{2,1,0:T(8,128)} %collective-permute-done.4, f32[16,64,512]{2,1,0:T(8,128)S(1)} %copy-done, s32[]{:T(128)S(6)} %select_n.22), kind=kLoop, calls=%fused_computation.2 | loop fusion | flops 262144 | bytes 3145732 | tf_op jit(solution)/shard_map/broadcast_in_dim | solution.py:114
  68.6 2.0 %copy.12 = f32[16,64,1,256]{3,2,1,0:T(1,128)} copy(f32[16,64,1,256]{3,1,0,2:T(8,128)S(1)} %add_bitcast_fusion) | data formatting | bytes 2097152 | tf_op jit(solution)/shard_map/broadcast_in_dim | solution.py:114
  (2 shorter events, 0.0 us)
Async XLA Ops:
  0.0 17.4 %copy-start.5 = (s32[16,1,8]{0,2,1:T(8,128)S(1)}, s32[16,1,8]{0,2,1:T(8,128)}, u32[]{:S(2)}) copy-start(s32[16,1,8]{0,2,1:T(8,128)} %param.9) | copy-start | bytes 1540
  2.8 15.4 %collective-permute-start.3 = (bf16[17,64,256]{2,1,0:T(8,128)(2,1)S(1)}, bf16[17,64,256]{2,1,0:T(8,128)(2,1)S(1)}, u32[]{:S(2)}, u32[]{:S(2)}) collective-permute-start(bf16[17,64,256]{2,1,0:T(8,128)(2,1)S(1)} %fusion.1), channel_id=1, source_target_pairs={{0,0},{5,1},{2,2},{7,3},{4,4},{1,5},{6,6},{3,7},{10,8},{15,9},{12,... | collective-permute-start | bytes 1671176 | tf_op jit(solution)/shard_map/ppermute | solution.py:101
  3.5 15.3 %collective-permute-start.2 = (bf16[17,64,256]{2,1,0:T(8,128)(2,1)S(1)}, bf16[17,64,256]{2,1,0:T(8,128)(2,1)S(1)}, u32[]{:S(2)}, u32[]{:S(2)}) collective-permute-start(bf16[17,64,256]{2,1,0:T(8,128)(2,1)S(1)} %fusion.1), channel_id=1, source_target_pairs={{0,0},{17,1},{10,2},{27,3},{20,4},{5,5},{30,6},{15,7},{8,8},{25,9}... | collective-permute-start | bytes 1671176 | tf_op jit(solution)/shard_map/ppermute | solution.py:100
  4.2 29.1 %collective-permute-start.1 = (bf16[17,64,256]{2,1,0:T(8,128)(2,1)S(1)}, bf16[17,64,256]{2,1,0:T(8,128)(2,1)S(1)}, u32[]{:S(2)}, u32[]{:S(2)}) collective-permute-start(bf16[17,64,256]{2,1,0:T(8,128)(2,1)S(1)} %fusion.1), channel_id=1, source_target_pairs={{2,0},{7,1},{4,2},{1,3},{6,4},{3,5},{0,6},{5,7},{12,8},{9,9},{14,1... | collective-permute-start | bytes 1671176 | tf_op jit(solution)/shard_map/ppermute | solution.py:101
  15.5 18.3 %collective-permute-start = (bf16[17,64,256]{2,1,0:T(8,128)(2,1)S(1)}, bf16[17,64,256]{2,1,0:T(8,128)(2,1)S(1)}, u32[]{:S(2)}, u32[]{:S(2)}) collective-permute-start(bf16[17,64,256]{2,1,0:T(8,128)(2,1)S(1)} %fusion.1), channel_id=1, source_target_pairs={{8,0},{25,1},{18,2},{3,3},{28,4},{13,5},{6,6},{23,7},{16,8},{1,9},... | collective-permute-start | bytes 1671176 | tf_op jit(solution)/shard_map/ppermute | solution.py:100
  18.2 17.9 %copy-start.1 = (bf16[17,64,256]{2,1,0:T(8,128)(2,1)}, bf16[17,64,256]{2,1,0:T(8,128)(2,1)S(1)}, u32[]{:S(2)}) copy-start(bf16[17,64,256]{2,1,0:T(8,128)(2,1)S(1)} %collective-permute-done.3.b_ref) | copy-start | bytes 1671172
  18.8 17.3 %copy-start.3 = (bf16[17,64,256]{2,1,0:T(8,128)(2,1)}, bf16[17,64,256]{2,1,0:T(8,128)(2,1)S(1)}, u32[]{:S(2)}) copy-start(bf16[17,64,256]{2,1,0:T(8,128)(2,1)S(1)} %collective-permute-done.2.a_ref) | copy-start | bytes 1671172
  33.3 16.2 %copy-start.2 = (bf16[17,64,256]{2,1,0:T(8,128)(2,1)}, bf16[17,64,256]{2,1,0:T(8,128)(2,1)S(1)}, u32[]{:S(2)}) copy-start(bf16[17,64,256]{2,1,0:T(8,128)(2,1)S(1)} %collective-permute-done.1.b_ref) | copy-start | bytes 1671172
  33.8 15.6 %copy-start.4 = (bf16[17,64,256]{2,1,0:T(8,128)(2,1)}, bf16[17,64,256]{2,1,0:T(8,128)(2,1)S(1)}, u32[]{:S(2)}) copy-start(bf16[17,64,256]{2,1,0:T(8,128)(2,1)S(1)} %collective-permute-done.a_ref) | copy-start | bytes 1671172
  62.8 4.3 %copy-start = (f32[16,64,512]{2,1,0:T(8,128)S(1)}, f32[16,64,512]{2,1,0:T(8,128)}, u32[]{:S(2)}) copy-start(f32[16,64,512]{2,1,0:T(8,128)} %shard_map.47) | copy-start | bytes 6291460
  64.3 2.9 %collective-permute-start.4 = (f32[16,64,256]{2,1,0:T(8,128)S(1)}, f32[16,64,256]{2,1,0:T(8,128)}, u32[]{:S(2)}, u32[]{:S(2)}) collective-permute-start(f32[16,64,256]{2,1,0:T(8,128)S(1)} %constant_dynamic-slice_fusion), channel_id=1, source_target_pairs={{0,1},{1,0},{2,3},{3,2},{4,5},{5,4},{6,7},{7,6},{8,9},{9,8},{10,11... | collective-permute-start | bytes 3145736 | tf_op jit(solution)/shard_map/ppermute | solution.py:110
